TPU v7x, 256 devices: a whole 4x4x8 slice. The times are simulated.
256 devices in a mesh: space: 32 (over z_lo, x, core), group: 8 (over y, z_hi).
Axes of the slice: x: 4, y: 4, z: 8 (z_hi: 2, z_lo: 4; z = z_hi * 4 + z_lo), core: 2. Of those that a mesh axis runs over, the one named last changes fastest.
Arguments:
- features: bfloat16 [8, 2048, 2432], P('group', 'space'), may hold values from -6 to 6
- positions: float32 [8, 3, 2048], P('group', None, 'space'), may hold values from 0 to 12
- cell_box: float32 [8, 3], P('group'), may hold values from 10 to 14
- send_rows: int32 [8, 2048], P('group', 'space'), may hold values from 0 to 63
- neighbours: int32 [8, 2048, 2], P('group', 'space'), may hold values from 0 to 127
- edge_mask: int32 [8, 2048, 2], P('group', 'space'), may hold values 0 or 1
- shift_ids: int32 [8, 2048, 2], P('group', 'space'), may hold values from 0 to 26
- target_forces: float32 [8, 3, 2048], P('group', None, 'space'), may hold values from -64 to 64
- w_zero: bfloat16 [896, 896], replicated, may hold values from -0.1875 to 0.1875
- w_real: bfloat16 [768, 768], replicated, may hold values from -0.15625 to 0.15625
- w_imag: bfloat16 [768, 768], replicated, may hold values from -0.15625 to 0.15625
- radial: float32 [600, 128], replicated, may hold values from -4 to 4
- readout: float32 [128], replicated, may hold values from -0.5 to 0.5
Outputs:
- forces: float32 [8, 3, 2048], P('group', None, 'space')
- grad_zero: float32 [896, 896], replicated
- grad_real: float32 [768, 768], replicated
- grad_imag: float32 [768, 768], replicated
- grad_radial: float32 [600, 128], replicated
- grad_readout: float32 [128], replicated
Inputs may be any that keep to these rules, and one draw needn't show every extreme that they name: `send_rows`: rows of the sending partition's own atoms. `neighbours`: rows of the partition's table of 128 atoms.
All inputs are finite; a program needn't handle non-finite values. No bound on the sum of `edge_mask` on one device may be relied on, other than what follows from the above.
Results may differ from a plain program's by a relative error of at most 0.0154.
Values may be sent and summed in bfloat16 or wider, within the bound.
No kernel may reach another device: no remote copies, remote signals or barrier semaphores. Data moves between devices by JAX's collectives and lax.ppermute only.
A program may use at most 128 MiB of HBM per device.

v0:
```python
import jax
import jax.numpy as jnp
from jax import lax
from jax.sharding import PartitionSpec as P

RANGE_TOP = 48.0


def padded(cells, sides, width):
    for axis, dim in sides:
        count = lax.axis_size(axis)
        head = lax.slice_in_dim(cells, 0, width, axis=dim)
        tail = lax.slice_in_dim(cells, cells.shape[dim] - width, cells.shape[dim], axis=dim)
        cells = jnp.concatenate(
            [
                lax.ppermute(tail, axis, [(i, (i + 1) % count) for i in range(count)]),
                cells,
                lax.ppermute(head, axis, [((i + 1) % count, i) for i in range(count)]),
            ],
            axis=dim,
        )
    return cells


def energy(params, table_feats, table_pos, neighbours, edge_mask, shift_ids, cell_box):
    w_zero, w_real, w_imag, radial, readout = params
    target_count, degree = neighbours.shape
    levels, channels = radial.shape
    flat_ids = neighbours.reshape(-1)
    edges = flat_ids.shape[0]
    shift_list = shift_ids.reshape(-1)
    offset = (
        jnp.stack([shift_list // 9 - 1, shift_list // 3 % 3 - 1, shift_list % 3 - 1]).astype(
            jnp.float32
        )
        * cell_box[:, None]
    )
    edge_vec = (
        jnp.take(table_pos, flat_ids, axis=1)
        + offset
        - jnp.repeat(table_pos[:, :target_count], degree, axis=1)
    )
    delta_one, delta_two, delta_three = (edge_vec[0], edge_vec[1], edge_vec[2])
    planar = jnp.sqrt(delta_one * delta_one + delta_two * delta_two + 1.0)
    radius = jnp.sqrt(planar * planar + delta_three * delta_three)
    cos_phi = (delta_one / planar)[:, None, None]
    sin_phi = (delta_two / planar)[:, None, None]
    cos_tilt = (delta_three / radius)[:, None, None]
    sin_tilt = (planar / radius)[:, None, None]
    spacing = RANGE_TOP / (levels - 1)
    centers = jnp.arange(levels, dtype=jnp.float32) * spacing
    basis_vals = jnp.exp(-jnp.square((radius[:, None] - centers[None, :]) / (2.0 * spacing)))
    radial_gain = jnp.dot(basis_vals, radial, precision=lax.Precision.HIGHEST)[:, None, :]
    source = (
        jnp.take(table_feats, flat_ids, axis=0).astype(jnp.float32).reshape(edges, 19, channels)
    )
    zero_part = source[:, 0:7]
    plus_part = source[:, 7:13]
    minus_part = source[:, 13:19]
    plus_turn = cos_phi * plus_part + sin_phi * minus_part
    minus_turn = cos_phi * minus_part - sin_phi * plus_part
    upper = zero_part[:, 1:]
    upper_tilt = cos_tilt * upper - sin_tilt * plus_turn
    plus_tilt = sin_tilt * upper + cos_tilt * plus_turn
    in_zero = (
        (jnp.concatenate([zero_part[:, 0:1], upper_tilt], 1) * radial_gain)
        .reshape(edges, 7 * channels)
        .astype(jnp.bfloat16)
    )
    in_plus = (plus_tilt * radial_gain).reshape(edges, 6 * channels).astype(jnp.bfloat16)
    in_minus = (minus_turn * radial_gain).reshape(edges, 6 * channels).astype(jnp.bfloat16)
    weight_zero = w_zero.astype(jnp.bfloat16)
    weight_real = w_real.astype(jnp.bfloat16)
    weight_imag = w_imag.astype(jnp.bfloat16)
    out_zero = jnp.dot(in_zero, weight_zero, preferred_element_type=jnp.float32).reshape(
        edges, 7, channels
    )
    out_plus = (
        jnp.dot(in_plus, weight_real, preferred_element_type=jnp.float32)
        - jnp.dot(in_minus, weight_imag, preferred_element_type=jnp.float32)
    ).reshape(edges, 6, channels)
    out_minus = (
        jnp.dot(in_plus, weight_imag, preferred_element_type=jnp.float32)
        + jnp.dot(in_minus, weight_real, preferred_element_type=jnp.float32)
    ).reshape(edges, 6, channels)
    upper_back = cos_tilt * out_zero[:, 1:] + sin_tilt * out_plus
    plus_back = cos_tilt * out_plus - sin_tilt * out_zero[:, 1:]
    plus_final = cos_phi * plus_back - sin_phi * out_minus
    minus_final = cos_phi * out_minus + sin_phi * plus_back
    message = jnp.concatenate([out_zero[:, 0:1], upper_back, plus_final, minus_final], 1)
    message = message * edge_mask.reshape(-1).astype(jnp.float32)[:, None, None]
    summed = message.reshape(target_count, degree, 19, channels).sum(axis=1) / degree
    updated = (
        table_feats[:target_count].astype(jnp.float32).reshape(target_count, 19, channels) + summed
    )
    invariant = updated[:, 0, :] + jnp.mean(updated * updated, axis=1)
    return jnp.sum(jax.nn.silu(invariant) * readout[None, :])


def per_device(
    features,
    positions,
    cell_box,
    send_rows,
    neighbours,
    edge_mask,
    shift_ids,
    target_forces,
    w_zero,
    w_real,
    w_imag,
    radial,
    readout,
):
    atom_feats = features[0]
    atom_pos = positions[0]
    box_sides = cell_box[0]
    sends = send_rows[0]
    neighbour_ids = neighbours[0]
    edge_live = edge_mask[0]
    shift_list = shift_ids[0]
    wanted = target_forces[0]
    own_count = atom_feats.shape[0]
    ghosts = sends.shape[0] // 2
    part_count = lax.axis_size("space")
    listed = jnp.take(atom_feats, sends, axis=0)
    beside_all = padded(listed, (("space", 0),), ghosts)
    table_feats = jnp.concatenate([atom_feats, beside_all[:ghosts], beside_all[3 * ghosts :]], 0)
    spots = jnp.take(atom_pos, sends, axis=1)
    nearby = padded(spots, (("space", 1),), ghosts)
    table_pos = jnp.concatenate([atom_pos, nearby[:, :ghosts], nearby[:, 3 * ghosts :]], 1)
    params = (
        w_zero.astype(jnp.float32),
        w_real.astype(jnp.float32),
        w_imag.astype(jnp.float32),
        radial,
        readout,
    )

    def position_grad(weights):
        return jax.grad(energy, 2)(
            weights, table_feats, table_pos, neighbour_ids, edge_live, shift_list, box_sides
        )

    grad_pos, pullback = jax.vjp(position_grad, params)
    ghost_grad = grad_pos[:, own_count:]
    backed = padded(ghost_grad, (("space", 1),), ghosts)
    returned = jnp.concatenate([backed[:, :ghosts], backed[:, 3 * ghosts :]], 1)
    onehot = (sends[:, None] == jnp.arange(own_count, dtype=jnp.int32)[None, :]).astype(jnp.float32)
    added = jnp.dot(returned, onehot, precision=lax.Precision.HIGHEST)
    forces = -(grad_pos[:, :own_count] + added)
    loss_weights = 2.0 * (forces - wanted) / (part_count * own_count)
    picked = jnp.take(loss_weights, sends, axis=1)
    shared = padded(picked, (("space", 1),), ghosts)
    table_u = jnp.concatenate([loss_weights, shared[:, :ghosts], shared[:, 3 * ghosts :]], 1)
    (grads,) = pullback(-table_u)
    grad_zero, grad_real, grad_imag, grad_radial, grad_readout = grads
    grad_zero, grad_real, grad_imag, grad_radial, grad_readout = lax.psum(
        (grad_zero, grad_real, grad_imag, grad_radial, grad_readout), ("space", "group")
    )
    return (forces[None], grad_zero, grad_real, grad_imag, grad_radial, grad_readout)


def solution(mesh):
    in_specs = (
        P("group", "space", None),
        P("group", None, "space"),
        P("group", None),
        P("group", "space"),
        P("group", "space", None),
        P("group", "space", None),
        P("group", "space", None),
        P("group", None, "space"),
        P(),
        P(),
        P(),
        P(),
        P(),
    )
    out_specs = (P("group", None, "space"), P(), P(), P(), P(), P())
    return jax.shard_map(
        per_device, mesh=mesh, in_specs=in_specs, out_specs=out_specs, check_vma=False
    )
```

profile of v0, /device:TPU:1, one launch (start us, length us, event | category | flops | bytes accessed | tf_op | source)
XLA Modules:
  0.0 544.8 jit_solution(3119229700067414699)
XLA Ops:
  10.1 2.7 collective-permute-start
  14.1 2.1 gather_fusion.1
  17.6 4.9 collective-permute-start.3
  26.5 3.6 copy.509
  35.4 2.5 multiply_convert_fusion.1
  42.8 2.1 convolution_subtract_fusion
  44.9 1.9 copy.513
  48.0 2.2 fusion.133
  51.9 6.4 %fusion.8 = f32[64,19,128]{2,0,1:T(8,128)S(1)} fusion(f32[64,2,6,128]{3,1,0,2:T(2,128)S(1)} %bitcast.340, f32[64,2,6,128]{3,1,0,2:T(2,128)S(1)} %bitcast.341, f32[64,2,6,128]{3,1,0,2:T(2,128)S(1)} %bitcast.342, f32[64,2,1,128]{3,1,0,2:T(2,128)S(1)} %bitcast.348, f32[64,2]{1,0:T(8,128)S(1)} %copy.519), kind=kLoop, calls=%fused_computation.27 | loop fusion | flops 1400832 | bytes 1868288 | tf_op jit(solution)/shard_map/jvp(jvp())/reduce_sum | solution.py:92
  63.5 1.9 copy.524
  65.4 2.3 convolution_convert_fusion.16
  68.9 1.7 copy.523
  70.7 2.3 fusion.19
  73.0 1.9 copy.530
  74.9 1.9 copy.531
  76.8 2.3 fusion.17
  79.1 1.9 copy.525
  81.1 1.9 copy.526
  83.0 2.7 multiply_reduce_fusion.14
  85.7 1.8 fusion.35
  87.5 1.8 copy.527
  89.3 2.9 fusion.11
  92.2 2.0 copy.528
  94.2 2.0 copy.529
  97.7 2.4 multiply_reduce_fusion.12
  105.0 1.6 reduce_sum.369
  109.3 2.9 scatter_fusion
  113.6 5.5 %collective-permute-start.5 = (f32[3,32]{0,1:T(8,128)}, f32[3,32]{0,1:T(8,128)}, u32[]{:S(2)}, u32[]{:S(2)}) collective-permute-start(f32[3,32]{0,1:T(8,128)} %get-tuple-element.133), channel_id=1, source_target_pairs={{8,0},{16,8},{24,16},{32,24},{40,32},{48,40},{56,48},{64,56},{72,6... | collective-permute-start | bytes 1160 | tf_op jit(solution)/shard_map/ppermute | solution.py:18
  124.6 1.5 fusion.88
  127.5 2.1 gather_fusion.5
  132.3 5.8 %collective-permute-start.7 = (f32[3,32]{1,0:T(4,128)}, f32[3,32]{1,0:T(4,128)}, u32[]{:S(2)}, u32[]{:S(2)}) collective-permute-start(f32[3,32]{1,0:T(4,128)} %get-tuple-element.143), channel_id=1, source_target_pairs={{8,0},{16,8},{24,16},{32,24},{40,32},{48,40},{56,48},{64,56},{72,6... | collective-permute-start | bytes 1160 | tf_op jit(solution)/shard_map/ppermute | solution.py:18
  138.1 1.8 copy.564
  143.2 2.2 gather_fusion.3
  148.3 1.6 neg.136
  151.4 1.8 fusion.48
  153.2 2.4 fusion.46
  156.4 2.9 multiply_reduce_fusion.7
  159.3 1.7 multiply_reduce_fusion.6
  161.0 1.8 copy.550
  162.8 2.1 fusion.138
  167.5 1.7 copy.551
  169.3 1.8 copy.547
  171.0 2.2 fusion.136
  175.1 1.9 copy.557
  177.0 1.9 copy.558
  178.9 2.2 fusion.10
  181.2 1.9 copy.552
  183.1 1.9 copy.553
  185.1 2.1 negate_add_fusion
  188.0 6.0 %fusion.9 = f32[64,19,128]{2,0,1:T(8,128)S(1)} fusion(f32[64,2,6,128]{3,1,0,2:T(2,128)S(1)} %bitcast.339, f32[64,2,6,128]{3,1,0,2:T(2,128)S(1)} %bitcast.337, f32[64,2,6,128]{3,1,0,2:T(2,128)S(1)} %bitcast.338, f32[64,2,1,128]{3,1,0,2:T(2,128)S(1)} %bitcast.328, f32[64,2]{1,0:T(8,128)S(1)} %copy-done.69), kind=kLoop, calls=%fused_computation.29 | loop fusion | flops 1400832 | bytes 1868288 | tf_op jit(solution)/shard_map/transpose(jvp(transpose(jvp())))/reduce_sum | solution.py:92
  205.0 1.5 fusion.141
  206.5 2.5 fusion.144
  210.5 1.5 fusion.145
  214.1 1.8 copy.561
  216.0 2.2 fusion.23
  218.2 1.9 copy.571
  220.2 1.9 copy.572
  225.5 2.8 fusion.12
  234.5 2.3 add_convert_fusion
  237.8 2.0 fusion.3
  239.9 2.0 fusion.7
  244.7 86.5 %psum.39 = f32[128]{0:T(128)} all-reduce(f32[128]{0:T(128)S(1)} %copy-done.128), channel_id=1, replica_groups=mesh['space'=32,'group'=8] {'space','group'}, use_global_device_ids=true, to_apply=%region_37.39 | all-reduce | flops 128 | bytes 1024 | tf_op jit(solution)/shard_map/psum | solution.py:158
  331.2 198.0 %all-reduce.14.cloned.1.call-done = (f32[896,896]{1,0:T(8,128)}, f32[768,768]{1,0:T(8,128)}, f32[768,768]{1,0:T(8,128)}, f32[600,128]{1,0:T(8,128)}) async-done(((f32[896,896]{1,0:T(8,128)}, f32[768,768]{1,0:T(8,128)}, f32[768,768]{1,0:T(8,128)}, f32[600,128]{1,0:T(8,128)}), (f32[896,896]{1,0:T(8,128)}, f32[768,768]{1,0:T(8,128)}, f32[768,768]{1,0:T(8,128)}, ...) | async-done | bytes 8237072 | tf_op jit(solution)/shard_map/psum | solution.py:158
  529.2 3.9 copy.590
  (416 shorter events, 94.7 us)
Async XLA Ops:
  7.2 31.0 %copy-start = (bf16[768,768]{1,0:T(8,128)(2,1)S(1)}, bf16[768,768]{1,0:T(8,128)(2,1)}, u32[]{:S(2)}) copy-start(bf16[768,768]{1,0:T(8,128)(2,1)} %param.25) | copy-start | bytes 3538948
  7.2 522.0 %all-reduce.14.cloned.1.call-start = ((), (), s32[]{:S(2)}) async-start(), calls=%async_computation | async-start | bytes 16474112 | tf_op jit(solution)/shard_map/psum | solution.py:158
  8.0 8.3 %copy-start.106 = (pred[64]{0:T(512)(128)(4,1)}, pred[64]{0:T(512)(128)(4,1)S(1)}, u32[]{:S(2)}) copy-start(pred[64]{0:T(512)(128)(4,1)S(1)} %compare_and_fusion) | copy-start | bytes 196
  10.1 20.1 %collective-permute-start = (f32[3,32]{0,1:T(8,128)S(1)}, f32[3,32]{0,1:T(8,128)S(1)}, u32[]{:S(2)}, u32[]{:S(2)}) collective-permute-start(f32[3,32]{0,1:T(8,128)S(1)} %get-tuple-element.134), channel_id=1, source_target_pairs={{0,8},{8,16},{16,24},{24,32},{32,40},{40,48},{48,56},{56,64},{64,7... | collective-permute-start | bytes 1160 | tf_op jit(solution)/shard_map/ppermute | solution.py:16
  12.8 17.4 %collective-permute-start.1 = (f32[3,32]{0,1:T(8,128)S(1)}, f32[3,32]{0,1:T(8,128)S(1)}, u32[]{:S(2)}, u32[]{:S(2)}) collective-permute-start(f32[3,32]{0,1:T(8,128)S(1)} %get-tuple-element.135), channel_id=1, source_target_pairs={{8,0},{16,8},{24,16},{32,24},{40,32},{48,40},{56,48},{64,56},{72,6... | collective-permute-start | bytes 1160 | tf_op jit(solution)/shard_map/ppermute | solution.py:18
  16.2 6.2 %copy-start.110 = (s32[1,64,2]{1,2,0:T(2,128)S(1)}, s32[1,64,2]{1,2,0:T(2,128)}, u32[]{:S(2)}) copy-start(s32[1,64,2]{1,2,0:T(2,128)} %param.21) | copy-start | bytes 1540
  16.2 6.3 %copy-start.126 = (s32[1,64,2]{1,2,0:T(2,128)S(1)}, s32[1,64,2]{1,2,0:T(2,128)}, u32[]{:S(2)}) copy-start(s32[1,64,2]{1,2,0:T(2,128)} %param.19) | copy-start | bytes 1540
  16.3 6.7 %copy-start.4 = (bf16[1,64,2432]{2,1,0:T(8,128)(2,1)S(1)}, bf16[1,64,2432]{2,1,0:T(8,128)(2,1)}, u32[]{:S(2)}) copy-start(bf16[1,64,2432]{2,1,0:T(8,128)(2,1)} %param.15) | copy-start | bytes 933892
  16.3 7.8 %copy-start.127 = (s32[1,64,2]{1,2,0:T(2,128)S(1)}, s32[1,64,2]{1,2,0:T(2,128)}, u32[]{:S(2)}) copy-start(s32[1,64,2]{1,2,0:T(2,128)} %param.20) | copy-start | bytes 1540
  16.4 15.5 %collective-permute-start.2 = (bf16[32,2432]{1,0:T(8,128)(2,1)S(1)}, bf16[32,2432]{1,0:T(8,128)(2,1)S(1)}, u32[]{:S(2)}, u32[]{:S(2)}) collective-permute-start(bf16[32,2432]{1,0:T(8,128)(2,1)S(1)} %get-tuple-element.129), channel_id=1, source_target_pairs={{0,8},{8,16},{16,24},{24,32},{32,40},{40,48},{48,56},{56,64},{64,7... | collective-permute-start | bytes 466952 | tf_op jit(solution)/shard_map/ppermute | solution.py:16
  17.6 14.4 %collective-permute-start.3 = (bf16[32,2432]{1,0:T(8,128)(2,1)S(1)}, bf16[32,2432]{1,0:T(8,128)(2,1)S(1)}, u32[]{:S(2)}, u32[]{:S(2)}) collective-permute-start(bf16[32,2432]{1,0:T(8,128)(2,1)S(1)} %get-tuple-element.130), channel_id=1, source_target_pairs={{8,0},{16,8},{24,16},{32,24},{40,32},{48,40},{56,48},{64,56},{72,6... | collective-permute-start | bytes 466952 | tf_op jit(solution)/shard_map/ppermute | solution.py:18
  22.5 8.5 %copy-start.89 = (f32[600]{0:T(1024)}, f32[600]{0:T(1024)S(1)}, u32[]{:S(2)}) copy-start(f32[600]{0:T(1024)S(1)} %iota_multiply_fusion) | copy-start | bytes 7204
  24.9 8.8 %copy-start.107 = (pred[128]{0:T(512)(128)(4,1)}, pred[128]{0:T(512)(128)(4,1)S(1)}, u32[]{:S(2)}) copy-start(pred[128]{0:T(512)(128)(4,1)S(1)} %compare_and_fusion.1) | copy-start | bytes 388
  24.9 5.2 copy-start.116
  25.0 7.0 %copy-start.104 = (s32[1024]{0:T(1024)}, s32[1024]{0:T(1024)S(1)}, u32[]{:S(2)}) copy-start(s32[1024]{0:T(1024)S(1)} %pad_clamp_fusion.1) | copy-start | bytes 12292
  26.3 25.6 %copy-start.68 = (f32[64,2]{1,0:T(8,128)}, f32[64,2]{1,0:T(8,128)S(1)}, u32[]{:S(2)}) copy-start(f32[64,2]{1,0:T(8,128)S(1)} %copy.519) | copy-start | bytes 1540
  26.5 4.4 copy-start.129
  26.5 4.5 copy-start.130
  31.9 3.5 copy-start.79
  33.9 132.1 %copy-start.54 = (f32[128,1,128]{2,0,1:T(8,128)}, f32[128,1,128]{2,0,1:T(8,128)S(1)}, u32[]{:S(2)}) copy-start(f32[128,1,128]{2,0,1:T(8,128)S(1)} %slice.114) | copy-start | bytes 196612
  35.3 12.7 %copy-start.48 = (bf16[128,7,128]{0,2,1:T(8,128)(2,1)}, bf16[128,7,128]{0,2,1:T(8,128)(2,1)S(1)}, u32[]{:S(2)}) copy-start(bf16[128,7,128]{0,2,1:T(8,128)(2,1)S(1)} %copy.508) | copy-start | bytes 688132
  38.0 4.8 copy-start.31
  51.9 6.4 %copy-start.45 = (f32[64,19,128]{2,1,0:T(8,128)S(1)}, f32[64,19,128]{2,1,0:T(8,128)}, u32[]{:S(2)}) copy-start(f32[64,19,128]{2,1,0:T(8,128)} %reshape.760) | copy-start | bytes 1867780
  97.6 3.1 copy-start.90
  97.6 3.1 copy-start.112
  97.6 3.1 copy-start.131
  97.6 3.8 copy-start.121
  97.6 3.8 copy-start.122
  97.6 3.8 copy-start.123
  97.6 3.8 copy-start.124
  97.6 3.8 copy-start.117
  97.7 3.8 copy-start.118
  97.7 3.8 copy-start.119
  97.7 3.8 copy-start.120
  113.6 8.3 %collective-permute-start.4 = (f32[3,32]{0,1:T(8,128)}, f32[3,32]{0,1:T(8,128)}, u32[]{:S(2)}, u32[]{:S(2)}) collective-permute-start(f32[3,32]{0,1:T(8,128)} %get-tuple-element.132), channel_id=1, source_target_pairs={{0,8},{8,16},{16,24},{24,32},{32,40},{40,48},{48,56},{56,64},{64,7... | collective-permute-start | bytes 1160 | tf_op jit(solution)/shard_map/ppermute | solution.py:16
  113.6 9.7 %collective-permute-start.5 = (f32[3,32]{0,1:T(8,128)}, f32[3,32]{0,1:T(8,128)}, u32[]{:S(2)}, u32[]{:S(2)}) collective-permute-start(f32[3,32]{0,1:T(8,128)} %get-tuple-element.133), channel_id=1, source_target_pairs={{8,0},{16,8},{24,16},{32,24},{40,32},{48,40},{56,48},{64,56},{72,6... | collective-permute-start | bytes 1160 | tf_op jit(solution)/shard_map/ppermute | solution.py:18
  132.3 7.6 %collective-permute-start.6 = (f32[3,32]{1,0:T(4,128)}, f32[3,32]{1,0:T(4,128)}, u32[]{:S(2)}, u32[]{:S(2)}) collective-permute-start(f32[3,32]{1,0:T(4,128)} %get-tuple-element.142), channel_id=1, source_target_pairs={{0,8},{8,16},{16,24},{24,32},{32,40},{40,48},{48,56},{56,64},{64,7... | collective-permute-start | bytes 1160 | tf_op jit(solution)/shard_map/ppermute | solution.py:16
  132.3 7.6 %collective-permute-start.7 = (f32[3,32]{1,0:T(4,128)}, f32[3,32]{1,0:T(4,128)}, u32[]{:S(2)}, u32[]{:S(2)}) collective-permute-start(f32[3,32]{1,0:T(4,128)} %get-tuple-element.143), channel_id=1, source_target_pairs={{8,0},{16,8},{24,16},{32,24},{40,32},{48,40},{56,48},{64,56},{72,6... | collective-permute-start | bytes 1160 | tf_op jit(solution)/shard_map/ppermute | solution.py:18
  149.9 6.4 %copy-start.3 = (f32[128,19,128]{2,0,1:T(8,128)S(1)}, f32[128,19,128]{2,0,1:T(8,128)}, u32[]{:S(2)}) copy-start(f32[128,19,128]{2,0,1:T(8,128)} %copy-done.2) | copy-start | bytes 3735556
  153.2 6.1 %copy-start.73 = (f32[128,128]{1,0:T(8,128)}, f32[128,128]{1,0:T(8,128)S(1)}, u32[]{:S(2)}) copy-start(f32[128,128]{1,0:T(8,128)S(1)} %fusion.48) | copy-start | bytes 196612
  156.3 3.0 copy-start.94
  156.3 3.0 copy-start.98
  156.3 3.0 copy-start.83
  156.3 3.0 copy-start.86
  156.3 3.0 copy-start.22
  156.3 3.0 copy-start.24
  171.0 3.0 copy-start.29
  171.0 3.0 copy-start.57
  181.1 3.9 copy-start.81
  181.1 3.9 copy-start.84
  181.2 3.9 copy-start.87
  181.2 3.9 copy-start.95
  181.2 3.9 copy-start.99
  203.2 3.3 copy-start.32
  205.0 4.0 copy-start.28
  205.0 4.0 copy-start.35
  206.5 4.0 copy-start.30
  209.0 3.0 copy-start.13
  209.0 3.1 copy-start.56
  209.0 3.0 copy-start.97
  209.0 3.0 copy-start.101
  218.2 3.9 copy-start.63
  234.5 3.3 copy-start.40
  529.2 4.0 copy-start.47
  (78 other events, 123.2 us)
Sparse Core Ops, SparseCore 0:
  243.6 285.5 all-reduce.13
where the time goes:
time: 552 us; the launch traced here: 545 us
  waiting for transfers between devices  198 us (36%)
  local copies, waits for them, and re-layouts  113 us (20%)
  blocking collectives  86.5 us (16%)
  matrix products  59.1 us (11%)
  other arithmetic  51.9 us (9%)
  starting transfers between devices  20.8 us (4%)
  between operations  15.8 us (3%)
    psum x1, waiting for transfers between devices, per_device(): lax.psum((grad_zero, grad_real, grad_imag, grad_radial, grad_readout), ('...  198 us
    psum x1, blocking collectives, per_device(): lax.psum((grad_zero, grad_real, grad_imag, grad_radial, grad_readout), ('...  86.5 us
    unnamed x273, local copies, waits for them, and re-layouts  28.9 us
    ppermute x4, starting transfers between devices, padded(): lax.ppermute(head, axis, [((i + 1) % count, i) for i in range(count)])  16.9 us
    dot_general x6, matrix products, energy(): jnp.dot(in_zero, weight_zero, preferred_element_type=jnp.float32)  12.9 us
    reduce_sum x2, other arithmetic, energy(): message.reshape(target_count, degree, 19, channels).sum(axis=1) / degree  12.4 us
  transfers between devices with their start and end apart: 9, of which 1 were waited for; matrix products, arithmetic and copies ran while one was open for 3% of the time, Pallas kernels for 0%

commit v1 on v0

--- a/solution.py
+++ b/solution.py
@@ -1,7 +1,7 @@
 import jax
 import jax.numpy as jnp
 from jax import lax
-from jax.sharding import PartitionSpec as P
+from jax.sharding import Mesh, PartitionSpec as P
 
 RANGE_TOP = 48.0
 
@@ -122,12 +122,12 @@
     wanted = target_forces[0]
     own_count = atom_feats.shape[0]
     ghosts = sends.shape[0] // 2
-    part_count = lax.axis_size("space")
+    part_count = lax.axis_size(SPACE)
     listed = jnp.take(atom_feats, sends, axis=0)
-    beside_all = padded(listed, (("space", 0),), ghosts)
+    beside_all = padded(listed, ((SPACE, 0),), ghosts)
     table_feats = jnp.concatenate([atom_feats, beside_all[:ghosts], beside_all[3 * ghosts :]], 0)
     spots = jnp.take(atom_pos, sends, axis=1)
-    nearby = padded(spots, (("space", 1),), ghosts)
+    nearby = padded(spots, ((SPACE, 1),), ghosts)
     table_pos = jnp.concatenate([atom_pos, nearby[:, :ghosts], nearby[:, 3 * ghosts :]], 1)
     params = (
         w_zero.astype(jnp.float32),
@@ -144,40 +144,77 @@
 
     grad_pos, pullback = jax.vjp(position_grad, params)
     ghost_grad = grad_pos[:, own_count:]
-    backed = padded(ghost_grad, (("space", 1),), ghosts)
+    backed = padded(ghost_grad, ((SPACE, 1),), ghosts)
     returned = jnp.concatenate([backed[:, :ghosts], backed[:, 3 * ghosts :]], 1)
     onehot = (sends[:, None] == jnp.arange(own_count, dtype=jnp.int32)[None, :]).astype(jnp.float32)
     added = jnp.dot(returned, onehot, precision=lax.Precision.HIGHEST)
     forces = -(grad_pos[:, :own_count] + added)
     loss_weights = 2.0 * (forces - wanted) / (part_count * own_count)
     picked = jnp.take(loss_weights, sends, axis=1)
-    shared = padded(picked, (("space", 1),), ghosts)
+    shared = padded(picked, ((SPACE, 1),), ghosts)
     table_u = jnp.concatenate([loss_weights, shared[:, :ghosts], shared[:, 3 * ghosts :]], 1)
     (grads,) = pullback(-table_u)
-    grad_zero, grad_real, grad_imag, grad_radial, grad_readout = grads
-    grad_zero, grad_real, grad_imag, grad_radial, grad_readout = lax.psum(
-        (grad_zero, grad_real, grad_imag, grad_radial, grad_readout), ("space", "group")
-    )
+    grad_zero, grad_real, grad_imag, grad_radial, grad_readout = all_sum(grads)
     return (forces[None], grad_zero, grad_real, grad_imag, grad_radial, grad_readout)
 
 
+SPACE = ("zl", "x", "c")
+GROUP = ("y", "zh")
+STAGES = (("c",), ("x", "y"), ("zh", "zl"))
+
+
+def all_sum(grads):
+    lanes = 128
+    sizes = [g.size for g in grads]
+    total = sum(sizes)
+    devices = 1
+    for stage in STAGES:
+        devices *= lax.axis_size(stage)
+    rows = -(-total // lanes)
+    rows = -(-rows // (devices * 16)) * devices * 16
+    flat = jnp.concatenate(
+        [g.reshape(-1) for g in grads] + [jnp.zeros((rows * lanes - total,), jnp.float32)]
+    )
+    part = flat.astype(jnp.bfloat16).reshape(rows, lanes)
+    for stage in STAGES:
+        count = lax.axis_size(stage)
+        got = lax.all_to_all(part, stage, 0, 0, tiled=True)
+        part = got.reshape(count, -1, lanes).astype(jnp.float32).sum(0).astype(jnp.bfloat16)
+    for stage in STAGES[::-1]:
+        count = lax.axis_size(stage)
+        spread = jnp.broadcast_to(part[None], (count,) + part.shape).reshape(-1, lanes)
+        part = lax.all_to_all(spread, stage, 0, 0, tiled=True)
+    flat = part.astype(jnp.float32).reshape(-1)
+    out, start = [], 0
+    for g, n in zip(grads, sizes):
+        out.append(flat[start : start + n].reshape(g.shape))
+        start += n
+    return out
+
+
 def solution(mesh):
+    space, group = mesh.shape["space"], mesh.shape["group"]
+    sub = Mesh(
+        mesh.devices.reshape(space // 8, 4, 2, group // 2, 2),
+        ("zl", "x", "c", "y", "zh"),
+    )
+    S, G = SPACE, GROUP
     in_specs = (
-        P("group", "space", None),
-        P("group", None, "space"),
-        P("group", None),
-        P("group", "space"),
-        P("group", "space", None),
-        P("group", "space", None),
-        P("group", "space", None),
-        P("group", None, "space"),
-        P(),
-        P(),
-        P(),
-        P(),
-        P(),
-    )
-    out_specs = (P("group", None, "space"), P(), P(), P(), P(), P())
+        P(G, S, None),
+        P(G, None, S),
+        P(G, None),
+        P(G, S),
+        P(G, S, None),
+        P(G, S, None),
+        P(G, S, None),
+        P(G, None, S),
+        P(),
+        P(),
+        P(),
+        P(),
+        P(),
+    )
+    out_specs = (P(G, None, S), P(), P(), P(), P(), P())
     return jax.shard_map(
-        per_device, mesh=mesh, in_specs=in_specs, out_specs=out_specs, check_vma=False
-    )
+        per_device, mesh=sub, in_specs=in_specs, out_specs=out_specs, check_vma=False
+    )

time: 552 us -> 398 us (0.72)
  waiting for transfers between devices: 198 us -> 23.8 us
  local copies, waits for them, and re-layouts: 113 us -> 132 us
  between operations: 15.8 us -> 2.49 us
  other arithmetic: 51.9 us -> 58.5 us
    psum x1 -> x0, waiting for transfers between devices: 198 us -> none  [per_device(): lax.psum((grad_zero, grad_real, grad_imag, grad_radial, grad_readout), ('...]
    all_to_all x0 -> x5, blocking collectives: none -> 88.8 us  [the longest x3 65 us: all_sum(): got = lax.all_to_all(part, stage, 0, 0, tiled=True)]
    psum x1 -> x0, blocking collectives: 86.5 us -> none  [per_device(): lax.psum((grad_zero, grad_real, grad_imag, grad_radial, grad_readout), ('...]
    all_to_all x0 -> x1, waiting for transfers between devices: none -> 23.8 us  [all_sum(): part = lax.all_to_all(spread, stage, 0, 0, tiled=True)]
    reshape x0 -> x6, local copies, waits for them, and re-layouts: none -> 19.2 us  [the longest x3 9.76 us: all_sum(): out.append(flat[start:start + n].reshape(g.shape))]
    reduce_sum x0 -> x3, other arithmetic: none -> 6.34 us  [all_sum(): got.reshape(count, -1, lanes).astype(jnp.float32).sum(0)]
    unnamed x273 -> x263, local copies, waits for them, and re-layouts: 28.9 us -> 24.1 us
  transfers between devices with their start and end apart: 9 -> 9, of which waited for: 1 -> 1; matrix products, arithmetic and copies ran while one was open for 3% -> 5% of each run, Pallas kernels for 0% -> 0%
where the time goes in v1:
time: 398 us; the launch traced here: 390 us
  local copies, waits for them, and re-layouts  132 us (33%)
  blocking collectives  88.8 us (22%)
  matrix products  60.9 us (15%)
  other arithmetic  58.5 us (15%)
  starting transfers between devices  24.4 us (6%)
  waiting for transfers between devices  23.8 us (6%)
    all_to_all x3, blocking collectives, all_sum(): got = lax.all_to_all(part, stage, 0, 0, tiled=True)  65 us
    unnamed x263, local copies, waits for them, and re-layouts  24.1 us
    all_to_all x2, blocking collectives, all_sum(): part = lax.all_to_all(spread, stage, 0, 0, tiled=True)  23.8 us
    all_to_all x1, waiting for transfers between devices, all_sum(): part = lax.all_to_all(spread, stage, 0, 0, tiled=True)  23.8 us
    ppermute x4, starting transfers between devices, padded(): lax.ppermute(head, axis, [((i + 1) % count, i) for i in range(count)])  16.8 us
    dot_general x6, matrix products, energy(): jnp.dot(in_minus, weight_imag, preferred_element_type=jnp.float32)  12.8 us
    reduce_sum x2, other arithmetic, energy(): message.reshape(target_count, degree, 19, channels).sum(axis=1) / degree  12.4 us
    dot_general x6, matrix products, energy(): jnp.dot(in_zero, weight_zero, preferred_element_type=jnp.float32)  11.6 us
  transfers between devices with their start and end apart: 9, of which 1 were waited for; matrix products, arithmetic and copies ran while one was open for 5% of the time, Pallas kernels for 0%

profile of v1, /device:TPU:1, one launch (start us, length us, event | category | flops | bytes accessed | tf_op | source)
XLA Modules:
  0.0 390.5 jit_solution(8925529627480036072)
XLA Ops:
  3.5 2.7 collective-permute-start
  7.6 2.1 gather_fusion.1
  11.0 4.9 %collective-permute-start.3 = (bf16[32,2432]{1,0:T(8,128)(2,1)S(1)}, bf16[32,2432]{1,0:T(8,128)(2,1)S(1)}, u32[]{:S(2)}, u32[]{:S(2)}) collective-permute-start(bf16[32,2432]{1,0:T(8,128)(2,1)S(1)} %get-tuple-element.128), channel_id=1, source_target_pairs={{8,0},{16,8},{24,16},{32,24},{40,32},{48,40},{56,48},{64,56},{72,6... | collective-permute-start | bytes 466952 | tf_op jit(solution)/shard_map/ppermute | solution.py:18
  19.9 3.6 copy.509
  28.8 2.5 multiply_convert_fusion.1
  36.2 2.1 convolution_subtract_fusion
  38.3 1.9 copy.513
  41.4 2.2 fusion.136
  45.3 6.4 %fusion.7 = f32[64,19,128]{2,0,1:T(8,128)S(1)} fusion(f32[64,2,6,128]{3,1,0,2:T(2,128)S(1)} %bitcast.356, f32[64,2,6,128]{3,1,0,2:T(2,128)S(1)} %bitcast.357, f32[64,2,6,128]{3,1,0,2:T(2,128)S(1)} %bitcast.358, f32[64,2,1,128]{3,1,0,2:T(2,128)S(1)} %bitcast.366, f32[64,2]{1,0:T(8,128)S(1)} %copy.519), kind=kLoop, calls=%fused_computation.26 | loop fusion | flops 1400832 | bytes 1868288 | tf_op jit(solution)/shard_map/jvp(jvp())/reduce_sum | solution.py:92
  56.9 1.9 copy.524
  58.8 2.3 convolution_convert_fusion.16
  64.1 2.3 fusion.21
  66.4 1.9 copy.530
  68.3 1.9 copy.531
  70.2 2.3 fusion.19
  72.5 1.9 copy.525
  74.4 1.9 copy.526
  76.4 2.7 multiply_reduce_fusion.14
  79.1 1.8 fusion.37
  80.9 1.8 copy.527
  82.7 2.9 fusion.10
  85.6 2.0 copy.528
  87.6 2.0 copy.529
  91.1 2.4 multiply_reduce_fusion.12
  102.8 2.9 scatter_fusion
  107.0 5.5 %collective-permute-start.5 = (f32[3,32]{0,1:T(8,128)}, f32[3,32]{0,1:T(8,128)}, u32[]{:S(2)}, u32[]{:S(2)}) collective-permute-start(f32[3,32]{0,1:T(8,128)} %get-tuple-element.131), channel_id=1, source_target_pairs={{8,0},{16,8},{24,16},{32,24},{40,32},{48,40},{56,48},{64,56},{72,6... | collective-permute-start | bytes 1160 | tf_op jit(solution)/shard_map/ppermute | solution.py:18
  121.0 2.1 gather_fusion.5
  125.8 5.7 %collective-permute-start.7 = (f32[3,32]{1,0:T(4,128)}, f32[3,32]{1,0:T(4,128)}, u32[]{:S(2)}, u32[]{:S(2)}) collective-permute-start(f32[3,32]{1,0:T(4,128)} %get-tuple-element.141), channel_id=1, source_target_pairs={{8,0},{16,8},{24,16},{32,24},{40,32},{48,40},{56,48},{64,56},{72,6... | collective-permute-start | bytes 1160 | tf_op jit(solution)/shard_map/ppermute | solution.py:18
  131.5 1.8 copy.564
  136.6 2.2 gather_fusion.3
  144.7 1.8 fusion.50
  146.6 2.4 fusion.48
  149.6 2.9 multiply_reduce_fusion.7
  156.0 2.1 fusion.141
  162.4 1.8 copy.547
  164.2 2.2 fusion.139
  168.3 1.9 copy.557
  170.2 1.9 copy.558
  172.1 2.2 fusion.9
  174.4 1.9 copy.552
  176.3 1.9 copy.553
  178.2 2.1 negate_add_fusion
  181.1 6.0 %fusion.8 = f32[64,19,128]{2,0,1:T(8,128)S(1)} fusion(f32[64,2,6,128]{3,1,0,2:T(2,128)S(1)} %bitcast.355, f32[64,2,6,128]{3,1,0,2:T(2,128)S(1)} %bitcast.353, f32[64,2,6,128]{3,1,0,2:T(2,128)S(1)} %bitcast.354, f32[64,2,1,128]{3,1,0,2:T(2,128)S(1)} %bitcast.344, f32[64,2]{1,0:T(8,128)S(1)} %copy-done.63), kind=kLoop, calls=%fused_computation.28 | loop fusion | flops 1400832 | bytes 1868288 | tf_op jit(solution)/shard_map/transpose(jvp(transpose(jvp())))/reduce_sum | solution.py:92
  198.6 2.5 fusion.147
  209.1 2.2 fusion.25
  215.0 2.0 fusion.11
  223.0 3.3 reshape.823
  226.2 3.5 fusion.6
  229.7 3.6 reshape.827
  233.3 3.5 fusion.3
  236.8 2.6 reshape.826
  247.1 2.3 dynamic-update-slice.5
  249.4 17.1 %all_to_all.42 = bf16[2,8192,128]{2,1,0:T(8,128)(2,1)} all-to-all(bf16[2,8192,128]{2,1,0:T(8,128)(2,1)} %bitcast.70), channel_id=1, replica_groups=mesh['zl'=4,'x'=4,'c'=2,'y'=4,'zh'=2] {'c'}, dimensions={0} | all-to-all | bytes 8388608 | tf_op jit(solution)/shard_map/all_to_all | solution.py:181
  266.5 4.4 %reduce_sum.419 = bf16[8192,128]{1,0:T(8,128)(2,1)S(1)} reduce(bf16[2,8192,128]{2,1,0:T(8,128)(2,1)} %all_to_all.42, bf16[]{:T(256)} %constant.143.clone.1), dimensions={0}, to_apply=%region_33.35 | reduce | flops 1048576 | bytes 6291458 | tf_op jit(solution)/shard_map/reduce_sum | solution.py:182
  271.0 30.6 %all_to_all.43 = bf16[16,512,128]{2,1,0:T(8,128)(2,1)} all-to-all(bf16[16,512,128]{2,1,0:T(8,128)(2,1)S(1)} %bitcast.300), channel_id=1, replica_groups=mesh['zl'=4,'x'=4,'c'=2,'y'=4,'zh'=2] {'x','y'}, dimensions={0} | all-to-all | bytes 4194304 | tf_op jit(solution)/shard_map/all_to_all | solution.py:181
  301.6 1.9 reduce_sum.420
  303.5 17.2 %all_to_all.44 = bf16[8,64,128]{2,1,0:T(8,128)(2,1)S(1)} all-to-all(bf16[8,64,128]{2,1,0:T(8,128)(2,1)S(1)} %bitcast.361), channel_id=1, replica_groups=mesh['zl'=4,'x'=4,'c'=2,'y'=4,'zh'=2] {'zh','zl'}, dimensions={0} | all-to-all | bytes 262144 | tf_op jit(solution)/shard_map/all_to_all | solution.py:181
  320.7 10.4 %all_to_all.45 = bf16[8,64,128]{2,1,0:T(8,128)(2,1)S(1)} all-to-all(bf16[8,64,128]{2,1,0:T(8,128)(2,1)S(1)} %broadcast_in_dim.162), channel_id=1, replica_groups=mesh['zl'=4,'x'=4,'c'=2,'y'=4,'zh'=2] {'zh','zl'}, dimensions={0} | all-to-all | bytes 262144 | tf_op jit(solution)/shard_map/all_to_all | solution.py:186
  332.9 3.9 all-to-all-start.4
  337.3 23.8 %all-to-all-done.4 = bf16[16,512,128]{2,1,0:T(8,128)(2,1)S(1)} async-done(((bf16[16,512,128]{2,1,0:T(8,128)(2,1)}), bf16[16,512,128]{2,1,0:T(8,128)(2,1)S(1)}, u32[]{:S(2)}, u32[]{:S(2)}) %all-to-all-start.4) | async-done | bytes 2097184 | tf_op jit(solution)/shard_map/all_to_all | solution.py:186
  361.4 13.4 %all_to_all.46 = bf16[2,8192,128]{2,1,0:T(8,128)(2,1)S(1)} all-to-all(bf16[2,8192,128]{2,1,0:T(8,128)(2,1)S(1)} %broadcast_in_dim.166), channel_id=1, replica_groups=mesh['zl'=4,'x'=4,'c'=2,'y'=4,'zh'=2] {'c'}, dimensions={0} | all-to-all | bytes 8388608 | tf_op jit(solution)/shard_map/all_to_all | solution.py:186
  376.9 1.8 slice.154
  382.1 4.7 %reshape.835 = f32[896,896]{1,0:T(8,128)} reshape(f32[6272,128]{1,0:T(8,128)} %slice.154) | data formatting | bytes 6422528 | tf_op jit(solution)/shard_map/reshape | solution.py:190
  386.8 3.4 reshape.836
  (428 shorter events, 118.4 us)
Async XLA Ops:
  0.6 31.0 %copy-start = (bf16[768,768]{1,0:T(8,128)(2,1)S(1)}, bf16[768,768]{1,0:T(8,128)(2,1)}, u32[]{:S(2)}) copy-start(bf16[768,768]{1,0:T(8,128)(2,1)} %param.25) | copy-start | bytes 3538948
  1.4 8.3 %copy-start.101 = (pred[64]{0:T(512)(128)(4,1)}, pred[64]{0:T(512)(128)(4,1)S(1)}, u32[]{:S(2)}) copy-start(pred[64]{0:T(512)(128)(4,1)S(1)} %compare_and_fusion) | copy-start | bytes 196
  3.5 20.0 %collective-permute-start = (f32[3,32]{0,1:T(8,128)S(1)}, f32[3,32]{0,1:T(8,128)S(1)}, u32[]{:S(2)}, u32[]{:S(2)}) collective-permute-start(f32[3,32]{0,1:T(8,128)S(1)} %get-tuple-element.132), channel_id=1, source_target_pairs={{0,8},{8,16},{16,24},{24,32},{32,40},{40,48},{48,56},{56,64},{64,7... | collective-permute-start | bytes 1160 | tf_op jit(solution)/shard_map/ppermute | solution.py:16
  6.2 17.4 %collective-permute-start.1 = (f32[3,32]{0,1:T(8,128)S(1)}, f32[3,32]{0,1:T(8,128)S(1)}, u32[]{:S(2)}, u32[]{:S(2)}) collective-permute-start(f32[3,32]{0,1:T(8,128)S(1)} %get-tuple-element.133), channel_id=1, source_target_pairs={{8,0},{16,8},{24,16},{32,24},{40,32},{48,40},{56,48},{64,56},{72,6... | collective-permute-start | bytes 1160 | tf_op jit(solution)/shard_map/ppermute | solution.py:18
  9.7 6.2 %copy-start.105 = (s32[1,64,2]{1,2,0:T(2,128)S(1)}, s32[1,64,2]{1,2,0:T(2,128)}, u32[]{:S(2)}) copy-start(s32[1,64,2]{1,2,0:T(2,128)} %param.21) | copy-start | bytes 1540
  9.7 6.2 %copy-start.122 = (s32[1,64,2]{1,2,0:T(2,128)S(1)}, s32[1,64,2]{1,2,0:T(2,128)}, u32[]{:S(2)}) copy-start(s32[1,64,2]{1,2,0:T(2,128)} %param.19) | copy-start | bytes 1540
  9.7 6.7 %copy-start.5 = (bf16[1,64,2432]{2,1,0:T(8,128)(2,1)S(1)}, bf16[1,64,2432]{2,1,0:T(8,128)(2,1)}, u32[]{:S(2)}) copy-start(bf16[1,64,2432]{2,1,0:T(8,128)(2,1)} %param.15) | copy-start | bytes 933892
  9.7 7.7 %copy-start.123 = (s32[1,64,2]{1,2,0:T(2,128)S(1)}, s32[1,64,2]{1,2,0:T(2,128)}, u32[]{:S(2)}) copy-start(s32[1,64,2]{1,2,0:T(2,128)} %param.20) | copy-start | bytes 1540
  9.9 15.5 %collective-permute-start.2 = (bf16[32,2432]{1,0:T(8,128)(2,1)S(1)}, bf16[32,2432]{1,0:T(8,128)(2,1)S(1)}, u32[]{:S(2)}, u32[]{:S(2)}) collective-permute-start(bf16[32,2432]{1,0:T(8,128)(2,1)S(1)} %get-tuple-element.127), channel_id=1, source_target_pairs={{0,8},{8,16},{16,24},{24,32},{32,40},{40,48},{48,56},{56,64},{64,7... | collective-permute-start | bytes 466952 | tf_op jit(solution)/shard_map/ppermute | solution.py:16
  11.0 14.3 %collective-permute-start.3 = (bf16[32,2432]{1,0:T(8,128)(2,1)S(1)}, bf16[32,2432]{1,0:T(8,128)(2,1)S(1)}, u32[]{:S(2)}, u32[]{:S(2)}) collective-permute-start(bf16[32,2432]{1,0:T(8,128)(2,1)S(1)} %get-tuple-element.128), channel_id=1, source_target_pairs={{8,0},{16,8},{24,16},{32,24},{40,32},{48,40},{56,48},{64,56},{72,6... | collective-permute-start | bytes 466952 | tf_op jit(solution)/shard_map/ppermute | solution.py:18
  15.9 8.5 %copy-start.84 = (f32[600]{0:T(1024)}, f32[600]{0:T(1024)S(1)}, u32[]{:S(2)}) copy-start(f32[600]{0:T(1024)S(1)} %iota_multiply_fusion) | copy-start | bytes 7204
  18.3 8.8 %copy-start.102 = (pred[128]{0:T(512)(128)(4,1)}, pred[128]{0:T(512)(128)(4,1)S(1)}, u32[]{:S(2)}) copy-start(pred[128]{0:T(512)(128)(4,1)S(1)} %compare_and_fusion.1) | copy-start | bytes 388
  18.3 5.2 %copy-start.108 = (s32[128]{0:T(128)}, s32[128]{0:T(128)S(1)}, u32[]{:S(2)}) copy-start(s32[128]{0:T(128)S(1)} %fusion.95) | copy-start | bytes 1540
  18.4 7.0 %copy-start.99 = (s32[1024]{0:T(1024)}, s32[1024]{0:T(1024)S(1)}, u32[]{:S(2)}) copy-start(s32[1024]{0:T(1024)S(1)} %pad_clamp_fusion.1) | copy-start | bytes 12292
  19.7 25.6 %copy-start.62 = (f32[64,2]{1,0:T(8,128)}, f32[64,2]{1,0:T(8,128)S(1)}, u32[]{:S(2)}) copy-start(f32[64,2]{1,0:T(8,128)S(1)} %copy.519) | copy-start | bytes 1540
  19.9 4.4 %copy-start.124 = (f32[1,3]{1,0:T(1,128)S(1)}, f32[1,3]{1,0:T(1,128)}, u32[]{:S(2)}) copy-start(f32[1,3]{1,0:T(1,128)} %param.17) | copy-start | bytes 40
  19.9 4.5 %copy-start.125 = (f32[600,128]{1,0:T(8,128)S(1)}, f32[600,128]{1,0:T(8,128)}, u32[]{:S(2)}) copy-start(f32[600,128]{1,0:T(8,128)} %param.26) | copy-start | bytes 921604
  25.3 3.5 copy-start.74
  27.3 131.9 %copy-start.48 = (f32[128,1,128]{2,0,1:T(8,128)}, f32[128,1,128]{2,0,1:T(8,128)S(1)}, u32[]{:S(2)}) copy-start(f32[128,1,128]{2,0,1:T(8,128)S(1)} %slice.142) | copy-start | bytes 196612
  28.7 12.7 %copy-start.45 = (bf16[128,7,128]{0,2,1:T(8,128)(2,1)}, bf16[128,7,128]{0,2,1:T(8,128)(2,1)S(1)}, u32[]{:S(2)}) copy-start(bf16[128,7,128]{0,2,1:T(8,128)(2,1)S(1)} %copy.508) | copy-start | bytes 688132
  31.4 4.8 %copy-start.30 = (bf16[128,6,128]{0,2,1:T(8,128)(2,1)}, bf16[128,6,128]{0,2,1:T(8,128)(2,1)S(1)}, u32[]{:S(2)}) copy-start(bf16[128,6,128]{0,2,1:T(8,128)(2,1)S(1)} %copy.512) | copy-start | bytes 589828
  45.2 6.4 %copy-start.42 = (f32[64,19,128]{2,1,0:T(8,128)S(1)}, f32[64,19,128]{2,1,0:T(8,128)}, u32[]{:S(2)}) copy-start(f32[64,19,128]{2,1,0:T(8,128)} %reshape.838) | copy-start | bytes 1867780
  91.0 3.1 copy-start.85
  91.0 3.1 copy-start.119
  91.0 3.1 copy-start.126
  91.0 3.8 copy-start.114
  91.0 3.8 copy-start.115
  91.0 3.8 copy-start.116
  91.0 3.8 copy-start.117
  91.0 3.8 copy-start.110
  91.1 3.8 copy-start.111
  91.1 3.8 copy-start.112
  91.1 3.8 copy-start.113
  107.0 8.3 %collective-permute-start.4 = (f32[3,32]{0,1:T(8,128)}, f32[3,32]{0,1:T(8,128)}, u32[]{:S(2)}, u32[]{:S(2)}) collective-permute-start(f32[3,32]{0,1:T(8,128)} %get-tuple-element.130), channel_id=1, source_target_pairs={{0,8},{8,16},{16,24},{24,32},{32,40},{40,48},{48,56},{56,64},{64,7... | collective-permute-start | bytes 1160 | tf_op jit(solution)/shard_map/ppermute | solution.py:16
  107.0 9.7 %collective-permute-start.5 = (f32[3,32]{0,1:T(8,128)}, f32[3,32]{0,1:T(8,128)}, u32[]{:S(2)}, u32[]{:S(2)}) collective-permute-start(f32[3,32]{0,1:T(8,128)} %get-tuple-element.131), channel_id=1, source_target_pairs={{8,0},{16,8},{24,16},{32,24},{40,32},{48,40},{56,48},{64,56},{72,6... | collective-permute-start | bytes 1160 | tf_op jit(solution)/shard_map/ppermute | solution.py:18
  125.8 7.4 %collective-permute-start.6 = (f32[3,32]{1,0:T(4,128)}, f32[3,32]{1,0:T(4,128)}, u32[]{:S(2)}, u32[]{:S(2)}) collective-permute-start(f32[3,32]{1,0:T(4,128)} %get-tuple-element.140), channel_id=1, source_target_pairs={{0,8},{8,16},{16,24},{24,32},{32,40},{40,48},{48,56},{56,64},{64,7... | collective-permute-start | bytes 1160 | tf_op jit(solution)/shard_map/ppermute | solution.py:16
  125.8 7.4 %collective-permute-start.7 = (f32[3,32]{1,0:T(4,128)}, f32[3,32]{1,0:T(4,128)}, u32[]{:S(2)}, u32[]{:S(2)}) collective-permute-start(f32[3,32]{1,0:T(4,128)} %get-tuple-element.141), channel_id=1, source_target_pairs={{8,0},{16,8},{24,16},{32,24},{40,32},{48,40},{56,48},{64,56},{72,6... | collective-permute-start | bytes 1160 | tf_op jit(solution)/shard_map/ppermute | solution.py:18
  143.3 6.3 %copy-start.4 = (f32[128,19,128]{2,0,1:T(8,128)S(1)}, f32[128,19,128]{2,0,1:T(8,128)}, u32[]{:S(2)}) copy-start(f32[128,19,128]{2,0,1:T(8,128)} %copy-done.3) | copy-start | bytes 3735556
  146.5 6.0 %copy-start.68 = (f32[128,128]{1,0:T(8,128)}, f32[128,128]{1,0:T(8,128)S(1)}, u32[]{:S(2)}) copy-start(f32[128,128]{1,0:T(8,128)S(1)} %fusion.50) | copy-start | bytes 196612
  149.5 3.0 copy-start.89
  149.6 3.0 copy-start.93
  149.6 3.0 copy-start.78
  149.6 3.0 copy-start.81
  149.6 3.0 copy-start.21
  164.2 3.0 copy-start.28
  164.2 3.0 copy-start.51
  174.3 3.8 copy-start.76
  174.3 3.8 copy-start.79
  174.4 3.8 copy-start.82
  174.4 3.8 copy-start.90
  174.4 3.8 copy-start.94
  197.1 4.0 %copy-start.35 = (bf16[128,6,128]{0,2,1:T(8,128)(2,1)S(1)}, bf16[128,6,128]{0,2,1:T(8,128)(2,1)}, u32[]{:S(2)}) copy-start(bf16[128,6,128]{0,2,1:T(8,128)(2,1)} %copy.550) | copy-start | bytes 589828
  197.1 4.0 %copy-start.36 = (bf16[128,6,128]{0,2,1:T(8,128)(2,1)S(1)}, bf16[128,6,128]{0,2,1:T(8,128)(2,1)}, u32[]{:S(2)}) copy-start(bf16[128,6,128]{0,2,1:T(8,128)(2,1)} %copy.523) | copy-start | bytes 589828
  198.6 4.1 %copy-start.29 = (bf16[128,6,128]{0,2,1:T(8,128)(2,1)S(1)}, bf16[128,6,128]{0,2,1:T(8,128)(2,1)}, u32[]{:S(2)}) copy-start(bf16[128,6,128]{0,2,1:T(8,128)(2,1)} %copy.551) | copy-start | bytes 589828
  201.1 3.1 copy-start.14
  201.1 3.1 copy-start.50
  201.1 3.1 copy-start.92
  201.1 3.1 copy-start.96
  205.3 3.7 copy-start.38
  223.0 3.3 copy-start.55
  229.7 3.6 copy-start.26
  332.9 3.9 copy-start.121
  332.9 28.2 %all-to-all-start.4 = ((bf16[16,512,128]{2,1,0:T(8,128)(2,1)}), bf16[16,512,128]{2,1,0:T(8,128)(2,1)S(1)}, u32[]{:S(2)}, u32[]{:S(2)}) async-start(bf16[16,512,128]{2,1,0:T(8,128)(2,1)} %broadcast_in_dim.164), calls=%async_computation.4 | async-start | bytes 4194304 | tf_op jit(solution)/shard_map/all_to_all | solution.py:186
  386.8 3.5 copy-start.1
  (73 other events, 106.8 us)
